TPU v7x, 256 devices: a whole 4x4x8 slice. The times are simulated.
256 devices in a mesh: seq: 32 (over z, x_hi, core), mp: 8 (over x_lo, y).
Axes of the slice: x: 4 (x_hi: 2, x_lo: 2; x = x_hi * 2 + x_lo), y: 4, z: 8, core: 2. Of those that a mesh axis runs over, the one named last changes fastest.
Arguments:
- queries: bfloat16 [4096, 8192], P('seq', 'mp'), may hold values from -200 to 200
- keys: bfloat16 [4096, 1024], P('seq', 'mp'), may hold values from -7 to 7
- values: float32 [4096, 1024], P('seq', 'mp'), may hold values from -24 to 24
- inputs_x: bfloat16 [4096, 8192], P('seq', 'mp'), may hold values from -6 to 6
- in_b: bfloat16 [4096, 128], P('seq'), may hold values from -6 to 6
- in_c: bfloat16 [4096, 128], P('seq'), may hold values from -6 to 6
- log_decay: float32 [4096, 64], P('seq', 'mp'), may hold values from -2 to 0
Outputs:
- grad_x: float32 [4096, 8192], P('seq', 'mp')
- grad_b: float32 [4096, 128], P(('seq', 'mp'))
- grad_c: float32 [4096, 128], P(('seq', 'mp'))
All inputs are finite; a program needn't handle non-finite values.
Results may differ from a plain program's by a relative error of at most 0.00035.
Values may be sent and summed in bfloat16 or wider, within the bound.
No kernel may reach another device: no remote copies, remote signals or barrier semaphores. Data moves between devices by JAX's collectives and lax.ppermute only.
A program may use at most 128 MiB of HBM per device.

v0:
```python
import math
import jax
import jax.numpy as jnp
from jax import lax
from jax.sharding import PartitionSpec as P

HEAD_WIDTH = 128
N = 128
HQ_DEV = 8
KV_DEV = 1
very_negative = -1e30
highest = lax.Precision.HIGHEST


def prefix(value, axis, join, neutral):
    count, mine = (lax.axis_size(axis), lax.axis_index(axis))
    pieces = jax.tree.map(lambda part: lax.all_gather(part, axis), value)
    subtotal = jax.tree.map(
        lambda part, zero: jnp.full_like(part, 0) + jnp.asarray(zero, part.dtype), value, neutral
    )

    def hop(position, subtotal):
        longer = join(subtotal, jax.tree.map(lambda part: part[position], pieces))
        return jax.tree.map(lambda new, old: jnp.where(position < mine, new, old), longer, subtotal)

    return lax.fori_loop(0, count - 1, hop, subtotal)


def chain_step(earlier, later):
    return (earlier[0] + later[0], jnp.exp(later[0])[:, None, None] * earlier[1] + later[1])


def attend_rows(current, query_head_rows, query_pos, key_piece, value_piece):
    row_top, denominator, mixture = current
    piece_rows = key_piece.shape[0]
    kv_heads = query_head_rows.shape[1]
    key_head_rows = key_piece.reshape(piece_rows, kv_heads, HEAD_WIDTH)
    value_head_rows = value_piece.reshape(piece_rows, kv_heads, HEAD_WIDTH)
    scores = jnp.einsum(
        "qkgd,nkd->qkgn", query_head_rows, key_head_rows, precision=highest
    ) / math.sqrt(HEAD_WIDTH)
    key_pos = jnp.arange(piece_rows, dtype=jnp.int32)
    allowed = (key_pos[None, :] <= query_pos[:, None])[:, None, None, :]
    scores = jnp.where(allowed, scores, very_negative)
    new_top = jnp.maximum(row_top, jnp.max(scores, axis=-1))
    weights = jnp.where(allowed, jnp.exp(scores - new_top[..., None]), 0.0)
    denominator = jnp.sum(weights, axis=-1)
    mixture = jnp.einsum("qkgn,nkd->qkgd", weights, value_head_rows, precision=highest)
    return (new_top, denominator, mixture)


def local(queries, keys, values, inputs_x, in_b, in_c, log_decay):
    row_count = queries.shape[0]
    group_width = HQ_DEV // KV_DEV
    seq_count = lax.axis_size("seq")
    own_index = lax.axis_index("seq")
    first_query = own_index * row_count
    query_sets = ((queries, first_query + jnp.arange(row_count, dtype=jnp.int32)),)
    head_sets = tuple(
        (
            rows.astype(jnp.float32).reshape(rows.shape[0], KV_DEV, group_width, HEAD_WIDTH)
            for rows, positions in query_sets
        )
    )
    pos_sets = tuple((positions for rows, positions in query_sets))
    start_state = tuple(
        (
            (
                jnp.full((positions.shape[0], KV_DEV, group_width), very_negative, jnp.float32),
                jnp.zeros((positions.shape[0], KV_DEV, group_width), jnp.float32),
                jnp.zeros((positions.shape[0], KV_DEV, group_width, HEAD_WIDTH), jnp.float32),
            )
            for positions in pos_sets
        )
    )
    key_piece = lax.all_gather(keys.astype(jnp.float32), "seq", axis=0, tiled=True)
    value_piece = lax.all_gather(values, "seq", axis=0, tiled=True)
    updated = []
    for current, query_head_rows, query_pos in zip(start_state, head_sets, pos_sets):

        def compute(state_now, query_head_rows=query_head_rows, query_pos=query_pos):
            return attend_rows(state_now, query_head_rows, query_pos, key_piece, value_piece)

        updated.append(compute(current))
    finished = tuple(updated)
    outputs = [
        (mixture / denominator[..., None]).reshape(mixture.shape[0], HQ_DEV, HEAD_WIDTH)
        for row_top, denominator, mixture in finished
    ]
    teacher_out = outputs[0]
    c_scale = 0.5 / math.sqrt(N * row_count * seq_count)
    student_x = inputs_x.astype(jnp.float32).reshape(row_count, HQ_DEV, HEAD_WIDTH)
    b_rows = in_b.astype(jnp.float32)
    c_rows = in_c.astype(jnp.float32) * c_scale
    cumulative = jnp.cumsum(log_decay, axis=0)
    totals = cumulative[-1]
    heads_first = cumulative.T
    causal = jnp.arange(row_count)[:, None] >= jnp.arange(row_count)[None, :]
    decays = jnp.exp(
        jnp.where(causal[None], heads_first[:, :, None] - heads_first[:, None, :], -jnp.inf)
    )
    inner_products = jnp.dot(in_c, in_b.T, preferred_element_type=jnp.float32) * c_scale
    mixing = decays * inner_products[None]
    rising = jnp.exp(cumulative)
    ending = jnp.exp(totals[None, :] - cumulative)
    local_state = jnp.einsum(
        "shp,sn->hpn", student_x * ending[:, :, None], b_rows, precision=highest
    )
    identity = (jnp.zeros_like(totals), jnp.zeros_like(local_state))
    prefix_log, state_in = prefix((totals, local_state), "seq", chain_step, identity)
    y_intra = jnp.einsum("hts,shp->thp", mixing, student_x, precision=highest)
    y_inter = jnp.einsum("tn,hpn->thp", c_rows, state_in, precision=highest) * rising[:, :, None]
    mismatch = y_intra + y_inter - teacher_out
    scaled_mismatch = mismatch * rising[:, :, None]
    local_grad = jnp.einsum("thp,tn->hpn", scaled_mismatch, c_rows, precision=highest)
    grad_pieces = lax.all_gather(local_grad[None], "seq", axis=0, tiled=True)
    log_pieces = lax.all_gather(prefix_log[None], "seq", axis=0, tiled=True)
    shard_ids = jnp.arange(grad_pieces.shape[0], dtype=jnp.int32)
    log_gaps = jnp.where(
        (shard_ids > own_index)[:, None], log_pieces - (prefix_log + totals)[None, :], -jnp.inf
    )
    later_grad = jnp.zeros_like(local_grad) + jnp.einsum(
        "ch,chpn->hpn", jnp.exp(log_gaps), grad_pieces, precision=highest
    )
    grad_x = jnp.einsum("hts,thp->shp", mixing, mismatch, precision=highest)
    grad_x = (
        grad_x
        + jnp.einsum("hpn,sn->shp", later_grad, b_rows, precision=highest) * ending[:, :, None]
    )
    products = jnp.einsum("thp,shp->hts", mismatch, student_x, precision=highest)
    weighted = decays * products
    grad_b = jnp.einsum("hts,tn->sn", weighted, c_rows, precision=highest)
    grad_b = grad_b + jnp.einsum(
        "shp,hpn->sn", student_x * ending[:, :, None], later_grad, precision=highest
    )
    grad_c = jnp.einsum("hts,sn->tn", weighted, b_rows, precision=highest)
    grad_c = grad_c + jnp.einsum("thp,hpn->tn", scaled_mismatch, state_in, precision=highest)
    summed_b, summed_c = (
        lax.psum_scatter(grad_b, "mp", scatter_dimension=0, tiled=True),
        lax.psum_scatter(grad_c, "mp", scatter_dimension=0, tiled=True),
    )
    return (grad_x.reshape(row_count, HQ_DEV * HEAD_WIDTH), summed_b, summed_c * c_scale)


def solution(mesh):
    in_specs = (
        P("seq", "mp"),
        P("seq", "mp"),
        P("seq", "mp"),
        P("seq", "mp"),
        P("seq", None),
        P("seq", None),
        P("seq", "mp"),
    )
    out_specs = (P("seq", "mp"), P(("seq", "mp"), None), P(("seq", "mp"), None))
    return jax.shard_map(local, mesh=mesh, in_specs=in_specs, out_specs=out_specs, check_vma=False)
```

profile of v0, /device:TPU:4, one launch (start us, length us, event | category | flops | bytes accessed | tf_op | source)
XLA Modules:
  0.0 594.7 jit_solution(6456232489600451371)
XLA Ops:
  7.2 1.4 convert_element_type.10
  11.7 1.9 fusion.35
  13.8 39.9 %all-gather.3 = f32[32,1,8]{2,1,0:T(1,128)S(1)} all-gather(f32[1,1,8]{2,1,0:T(1,128)S(1)} %get-tuple-element.162), channel_id=1, replica_groups=mesh['seq'=32,'mp'=8] {'seq'}, dimensions={0}, use_global_device_ids=true | all-gather | bytes 1056 | tf_op jit(solution)/shard_map/all_gather | solution.py:17
  55.7 35.7 %all-gather.9.cloned.1.call-done = f32[4096,128]{1,0:T(8,128)} async-done(((f32[128,128]{1,0:T(8,128)}), f32[4096,128]{1,0:T(8,128)}) %all-gather.9.cloned.1.call-update) | async-done | bytes 2097168 | tf_op jit(solution)/shard_map/all_gather | solution.py:76
  91.3 10.0 %fusion.5 = (f32[128,8]{0,1:T(8,128)S(1)}, f32[4096,128,8]{1,0,2:T(8,128)S(1)}) fusion(pred[128,4096]{0,1:T(8,128)(4,1)S(1)} %iota_compare_fusion, f32[4096,128]{1,0:T(8,128)} %all-gather.9.cloned.1.call-done, bf16[128,1024]{1,0:T(8,128)(2,1)S(1)} %copy-done), kind=kOutput, calls=%fused_computation.12 | convolution fusion | flops 6455032832 | bytes 19664896 | tf_op jit(solution)/shard_map/qkgd,nkd->qkgn/dot_general | solution.py:39
  101.4 5.7 copy-done.1
  107.1 4.0 fusion.6
  111.1 59.6 %all-gather.11.cloned.1.call-done = f32[4096,128]{1,0:T(8,128)} async-done(((f32[128,128]{1,0:T(8,128)}), f32[4096,128]{1,0:T(8,128)}) %all-gather.11.cloned.1.call-update) | async-done | bytes 2097168 | tf_op jit(solution)/shard_map/all_gather | solution.py:77
  170.7 32.2 %fusion.30 = f32[128,8,128]{2,0,1:T(8,128)S(1)} fusion(f32[4096,128]{1,0:T(8,128)} %all-gather.11.cloned.1.call-done, f32[4096,128,8]{1,0,2:T(8,128)} %copy-done.1, f32[128,8]{0,1:T(8,128)S(1)} %broadcast_maximum_fusion, pred[128,4096]{0,1:T(8,128)(4,1)S(1)} %iota_compare_fusion, f32[128,8]{0,1:T(8,128)S(1)} %fusion.6), kind=kOutput, calls=%fused_computation.40 | convolution fusion | flops 6459359232 | bytes 19931136 | tf_op jit(solution)/shard_map/qkgn,nkd->qkgd/dot_general | solution.py:48
  203.0 105.5 %all-gather.13.cloned.1.call-done = f32[256,128,128]{2,1,0:T(8,128)} async-done(((f32[8,128,128]{2,1,0:T(8,128)}), f32[256,128,128]{2,1,0:T(8,128)}) %all-gather.13.cloned.1.call-update) | async-done | bytes 16777232 | tf_op jit(solution)/shard_map/all_gather | solution.py:17
  308.5 37.8 %while.16 = (s32[]{:T(128)}, f32[8]{0:T(128)S(1)}, f32[8,128,128]{2,1,0:T(8,128)S(1)}, s32[]{:T(128)}, f32[32,8]{1,0:T(8,128)S(1)}, /*index=5*/f32[32,8,128,128]{3,2,1,0:T(8,128)}, s32[]{:T(128)}, s32[]{:T(128)}) while((s32[]{:T(128)}, f32[8]{0:T(128)S(1)}, f32[8,128,128]{2,1,0:T(8,128)S(1)}, s32[]{:T(128)}, ...), condition=%wide.region_2.3_spmd.clone, body=%wide.region_1.2_spmd.clone.sunk | while | flops 524316 | bytes 1573139 | solution.py:26
  309.7 1.2 fusion.91
  310.9 1.2 fusion.91
  312.2 1.2 fusion.91
  313.4 1.2 fusion.91
  321.9 1.2 fusion.91
  323.2 1.2 fusion.91
  324.4 1.2 fusion.91
  325.6 1.2 fusion.91
  326.8 1.2 fusion.91
  328.0 1.2 fusion.91
  329.3 1.2 fusion.91
  330.5 1.2 fusion.91
  331.7 1.2 fusion.91
  345.1 1.2 fusion.91
  349.0 1.9 fusion.40
  352.5 63.4 %all-reduce = f32[256]{0:T(256)S(1)} all-reduce(f32[256]{0:T(256)S(1)} %dynamic-update-slice), channel_id=3, replica_groups=mesh['seq'=32,'mp'=8] {'seq'}, use_global_device_ids=true, to_apply=%add | all-reduce | flops 256 | bytes 2048
  416.2 1.2 convolution_bitcast_fusion.2
  417.4 1.3 broadcast_multiply_fusion
  418.7 106.9 %all-gather.15.cloned.1.call-done = f32[256,128,128]{2,1,0:T(8,128)} async-done(((f32[8,128,128]{2,1,0:T(8,128)}), f32[256,128,128]{2,1,0:T(8,128)}) %all-gather.15.cloned.1.call-update) | async-done | bytes 16777232 | tf_op jit(solution)/shard_map/all_gather | solution.py:116
  525.6 21.8 %fusion.3 = f32[8,1,128,128]{3,1,2,0:T(1,128)S(1)} fusion(f32[32,8,1,1]{0,2,3,1:T(1,128)S(1)} %copy.56, f32[32,8,128,128]{3,2,1,0:T(8,128)} %bitcast.129), kind=kOutput, calls=%fused_computation.9 | convolution fusion | flops 50331648 | bytes 17302528 | tf_op jit(solution)/shard_map/ch,chpn->hpn/dot_general | solution.py:122
  550.7 37.1 %reduce-scatter.3.cloned.1.call-done = f32[16,128]{1,0:T(8,128)} async-done(((f32[128,128]{1,0:T(8,128)}), f32[16,128]{1,0:T(8,128)}) %reduce-scatter.3.cloned.1.call-update) | async-done | bytes 8208 | tf_op jit(solution)/shard_map/reduce_scatter | solution.py:139
  (102 shorter events, 32.8 us)
Async XLA Ops:
  7.2 84.2 %copy-start = (bf16[128,1024]{1,0:T(8,128)(2,1)S(1)}, bf16[128,1024]{1,0:T(8,128)(2,1)}, u32[]{:S(2)}) copy-start(bf16[128,1024]{1,0:T(8,128)(2,1)} %param.9) | copy-start | bytes 786436
  7.2 84.2 %all-gather.9.cloned.1.call-start = ((), (), s32[]{:S(2)}) async-start(), calls=%async_computation.2 | async-start | bytes 2162688 | tf_op jit(solution)/shard_map/all_gather | solution.py:76
  8.7 162.1 %all-gather.11.cloned.1.call-start = ((), (), s32[]{:S(2)}) async-start(), calls=%async_computation.3 | async-start | bytes 2162688 | tf_op jit(solution)/shard_map/all_gather | solution.py:77
  9.4 299.1 %all-gather.13.cloned.1.call-start = ((), (), s32[]{:S(2)}) async-start(), calls=%async_computation.6 | async-start | bytes 17301504 | tf_op jit(solution)/shard_map/all_gather | solution.py:17
  13.6 403.8 %reduce-scatter.5.cloned.1.call-start = ((), (), s32[]{:S(2)}) async-start(), calls=%async_computation.5 | async-start | bytes 73728 | tf_op jit(solution)/shard_map/reduce_scatter | solution.py:140
  101.3 5.7 copy-start.1
  111.1 235.2 %copy-start.2 = (bf16[128,128]{1,0:T(8,128)(2,1)S(1)}, bf16[128,128]{1,0:T(8,128)(2,1)}, u32[]{:S(2)}) copy-start(bf16[128,128]{1,0:T(8,128)(2,1)} %param.14) | copy-start | bytes 98308
  111.1 237.0 %copy-start.3 = (bf16[128,128]{1,0:T(8,128)(2,1)S(1)}, bf16[128,128]{1,0:T(8,128)(2,1)}, u32[]{:S(2)}) copy-start(bf16[128,128]{1,0:T(8,128)(2,1)} %param.13) | copy-start | bytes 98308
  111.1 239.9 %copy-start.4 = (u32[256]{0:T(256)S(1)}, u32[256]{0:T(256)}, u32[]{:S(2)}) copy-start(u32[256]{0:T(256)} %constant.52) | copy-start | bytes 3076
  348.9 176.7 %all-gather.15.cloned.1.call-start = ((), (), s32[]{:S(2)}) async-start(), calls=%async_computation.7 | async-start | bytes 17301504 | tf_op jit(solution)/shard_map/all_gather | solution.py:116
  350.9 236.9 %reduce-scatter.3.cloned.1.call-start = ((), (), s32[]{:S(2)}) async-start(), calls=%async_computation.4 | async-start | bytes 73728 | tf_op jit(solution)/shard_map/reduce_scatter | solution.py:139
Sparse Core Ops, SparseCore 0:
  10.8 80.4 all-gather.8
  94.1 76.5 all-gather.10
  174.1 134.3 all-gather.12
  349.0 38.3 reduce-scatter.4
  391.0 134.4 all-gather.14
  549.5 38.3 reduce-scatter.2
where the time goes:
time: 597 us; the launch traced here: 595 us
  waiting for transfers between devices  346 us (58%)
  blocking collectives  103 us (17%)
  matrix products  75.6 us (13%)
  other arithmetic  44.4 us (7%)
  between operations  15 us (3%)
  local copies, waits for them, and re-layouts  9.81 us (2%)
    all_gather x1, waiting for transfers between devices, local(): grad_pieces = lax.all_gather(local_grad[None], 'seq', axis=0, tiled=True)  107 us
    all_gather x1, waiting for transfers between devices, prefix(): pieces = jax.tree.map(lambda part: lax.all_gather(part, axis), value)  105 us
    unnamed x1, blocking collectives  63.4 us
    all_gather x1, waiting for transfers between devices, local(): value_piece = lax.all_gather(values, 'seq', axis=0, tiled=True)  59.6 us
    all_gather x1, blocking collectives, prefix(): pieces = jax.tree.map(lambda part: lax.all_gather(part, axis), value)  39.9 us
    reduce_scatter x1, waiting for transfers between devices, local(): lax.psum_scatter(grad_b, 'mp', scatter_dimension=0, tiled=True)  37.1 us
    select_n x31, other arithmetic, hop(): jnp.where(position < mine, new, old)  36.4 us
    all_gather x1, waiting for transfers between devices, local(): lax.all_gather(keys.astype(jnp.float32), 'seq', axis=0, tiled=True)  35.7 us
  transfers between devices with their start and end apart: 6, of which 5 were waited for; matrix products, arithmetic and copies ran while one was open for 10% of the time, Pallas kernels for 0%

commit v1 on v0

--- a/solution.py
+++ b/solution.py
@@ -10,6 +10,11 @@
 KV_DEV = 1
 very_negative = -1e30
 highest = lax.Precision.HIGHEST
+
+
+def all_by_exchange(array, axis, dim):
+    sent = jnp.stack([array] * lax.axis_size(axis))
+    return jnp.concatenate(lax.all_to_all(sent, axis, 0, 0), axis=dim)
 
 
 def prefix(value, axis, join, neutral):
@@ -74,7 +79,7 @@
         )
     )
     key_piece = lax.all_gather(keys.astype(jnp.float32), "seq", axis=0, tiled=True)
-    value_piece = lax.all_gather(values, "seq", axis=0, tiled=True)
+    value_piece = all_by_exchange(values, "seq", 0)
     updated = []
     for current, query_head_rows, query_pos in zip(start_state, head_sets, pos_sets):
 

time: 597 us -> 525 us (0.88)
  waiting for transfers between devices: 346 us -> 219 us
  blocking collectives: 103 us -> 144 us
  starting transfers between devices: 0.24 us -> 11.8 us
    all_gather x1 -> x0, waiting for transfers between devices: 59.6 us -> none  [local(): value_piece = lax.all_gather(values, 'seq', axis=0, tiled=True)]
    all_gather x1, blocking collectives: 39.9 us -> 80.8 us  [prefix(): pieces = jax.tree.map(lambda part: lax.all_gather(part, axis), value)]
    all_gather x1, waiting for transfers between devices: 35.7 us -> 0.02 us  [local(): lax.all_gather(keys.astype(jnp.float32), 'seq', axis=0, tiled=True)]
    all_gather x1, waiting for transfers between devices: 105 us -> 75.1 us  [prefix(): pieces = jax.tree.map(lambda part: lax.all_gather(part, axis), value)]
    all_to_all x0 -> x1, starting transfers between devices: none -> 11.6 us  [all_by_exchange(): return jnp.concatenate(lax.all_to_all(sent, axis, 0, 0), axis=dim)]
  transfers between devices with their start and end apart: 6 -> 6, of which waited for: 5 -> 3; matrix products, arithmetic and copies ran while one was open for 10% -> 12% of each run, Pallas kernels for 0% -> 0%
where the time goes in v1:
time: 525 us; the launch traced here: 523 us
  waiting for transfers between devices  219 us (42%)
  blocking collectives  144 us (27%)
  matrix products  75.7 us (14%)
  other arithmetic  44.4 us (8%)
  between operations  14.7 us (3%)
  local copies, waits for them, and re-layouts  12.2 us (2%)
  starting transfers between devices  11.8 us (2%)
    all_gather x1, waiting for transfers between devices, local(): grad_pieces = lax.all_gather(local_grad[None], 'seq', axis=0, tiled=True)  107 us
    all_gather x1, blocking collectives, prefix(): pieces = jax.tree.map(lambda part: lax.all_gather(part, axis), value)  80.8 us
    all_gather x1, waiting for transfers between devices, prefix(): pieces = jax.tree.map(lambda part: lax.all_gather(part, axis), value)  75.1 us
    unnamed x1, blocking collectives  63.4 us
    reduce_scatter x1, waiting for transfers between devices, local(): lax.psum_scatter(grad_b, 'mp', scatter_dimension=0, tiled=True)  37.1 us
    select_n x31, other arithmetic, hop(): jnp.where(position < mine, new, old)  36.4 us
    dot_general x1, matrix products, attend_rows(): jnp.einsum('qkgn,nkd->qkgd', weights, value_head_rows, precision=highest)  32.3 us
    dot_general x1, matrix products, local(): jnp.einsum('ch,chpn->hpn', jnp.exp(log_gaps), grad_pieces, precision=high...  21.8 us
  transfers between devices with their start and end apart: 6, of which 3 were waited for; matrix products, arithmetic and copies ran while one was open for 12% of the time, Pallas kernels for 0%

profile of v1, /device:TPU:4, one launch (start us, length us, event | category | flops | bytes accessed | tf_op | source)
XLA Modules:
  0.0 523.2 jit_solution(4304742484922876812)
XLA Ops:
  7.2 1.4 convert_element_type.10
  10.9 2.0 fusion.28
  12.9 2.4 stack.2
  15.3 11.6 %all-to-all-start = ((f32[32,128,128]{2,1,0:T(8,128)}), f32[32,128,128]{2,1,0:T(8,128)}, u32[]{:S(2)}, u32[]{:S(2)}) async-start(f32[32,128,128]{2,1,0:T(8,128)} %stack.2), calls=%async_computation | async-start | bytes 4194304 | tf_op jit(solution)/shard_map/all_to_all | solution.py:17
  27.2 80.8 %all-gather.3 = f32[32,1,8]{2,1,0:T(1,128)S(1)} all-gather(f32[1,1,8]{2,1,0:T(1,128)S(1)} %get-tuple-element.162), channel_id=1, replica_groups=mesh['seq'=32,'mp'=8] {'seq'}, dimensions={0}, use_global_device_ids=true | all-gather | bytes 1056 | tf_op jit(solution)/shard_map/all_gather | solution.py:22
  110.0 10.0 %fusion.5 = (f32[128,8]{0,1:T(8,128)S(1)}, f32[4096,128,8]{1,0,2:T(8,128)S(1)}) fusion(pred[128,4096]{0,1:T(8,128)(4,1)S(1)} %iota_compare_fusion, f32[4096,128]{1,0:T(8,128)} %all-gather.8.cloned.1.call-done, bf16[128,1024]{1,0:T(8,128)(2,1)S(1)} %copy-done), kind=kOutput, calls=%fused_computation.12 | convolution fusion | flops 6455032832 | bytes 19664896 | tf_op jit(solution)/shard_map/qkgd,nkd->qkgn/dot_general | solution.py:44
  120.1 5.7 %copy-done.1 = f32[4096,128,8]{1,0,2:T(8,128)} copy-done((f32[4096,128,8]{1,0,2:T(8,128)}, f32[4096,128,8]{1,0,2:T(8,128)S(1)}, u32[]{:S(2)}) %copy-start.1) | copy-done | bytes 16777240
  125.8 4.0 fusion.6
  129.9 32.3 %fusion.25 = f32[128,8,128]{2,0,1:T(8,128)S(1)} fusion(f32[4096,128,1]{1,0,2:T(8,128)} %bitcast.14, f32[4096,128,8]{1,0,2:T(8,128)} %copy-done.1, f32[128,8]{0,1:T(8,128)S(1)} %broadcast_maximum_fusion, pred[128,4096]{0,1:T(8,128)(4,1)S(1)} %iota_compare_fusion, f32[128,8]{0,1:T(8,128)S(1)} %fusion.6), kind=kOutput, calls=%fused_computation.39 | convolution fusion | flops 6459359232 | bytes 19931136 | tf_op jit(solution)/shard_map/qkgn,nkd->qkgd/dot_general | solution.py:53
  162.1 75.1 %all-gather.10.cloned.1.call-done = f32[256,128,128]{2,1,0:T(8,128)} async-done(((f32[8,128,128]{2,1,0:T(8,128)}), f32[256,128,128]{2,1,0:T(8,128)}) %all-gather.10.cloned.1.call-update) | async-done | bytes 16777232 | tf_op jit(solution)/shard_map/all_gather | solution.py:22
  237.3 37.8 %while.16 = (s32[]{:T(128)}, f32[8]{0:T(128)S(1)}, f32[8,128,128]{2,1,0:T(8,128)S(1)}, s32[]{:T(128)}, f32[32,8]{1,0:T(8,128)S(1)}, /*index=5*/f32[32,8,128,128]{3,2,1,0:T(8,128)}, s32[]{:T(128)}, s32[]{:T(128)}) while((s32[]{:T(128)}, f32[8]{0:T(128)S(1)}, f32[8,128,128]{2,1,0:T(8,128)S(1)}, s32[]{:T(128)}, ...), condition=%wide.region_2.3_spmd.clone, body=%wide.region_1.2_spmd.clone.sunk | while | flops 524316 | bytes 1573147 | solution.py:31
  238.5 1.2 fusion.85
  239.7 1.2 fusion.85
  248.3 1.2 fusion.85
  249.5 1.2 fusion.85
  250.7 1.2 fusion.85
  251.9 1.2 fusion.85
  253.2 1.2 fusion.85
  254.4 1.2 fusion.85
  255.6 1.2 fusion.85
  256.8 1.2 fusion.85
  258.0 1.2 fusion.85
  271.5 1.2 fusion.85
  272.7 1.2 fusion.85
  273.9 1.2 fusion.85
  277.8 1.9 fusion.33
  281.3 63.4 %all-reduce = f32[256]{0:T(256)S(1)} all-reduce(f32[256]{0:T(256)S(1)} %dynamic-update-slice), channel_id=3, replica_groups=mesh['seq'=32,'mp'=8] {'seq'}, use_global_device_ids=true, to_apply=%add | all-reduce | flops 256 | bytes 2048
  345.0 1.2 convolution_bitcast_fusion.2
  346.2 1.3 broadcast_multiply_fusion
  347.5 106.9 %all-gather.12.cloned.1.call-done = f32[256,128,128]{2,1,0:T(8,128)} async-done(((f32[8,128,128]{2,1,0:T(8,128)}), f32[256,128,128]{2,1,0:T(8,128)}) %all-gather.12.cloned.1.call-update) | async-done | bytes 16777232 | tf_op jit(solution)/shard_map/all_gather | solution.py:121
  454.4 21.8 %fusion.3 = f32[8,1,128,128]{3,1,2,0:T(1,128)S(1)} fusion(f32[32,8,1,1]{0,2,3,1:T(1,128)S(1)} %copy.56, f32[32,8,128,128]{3,2,1,0:T(8,128)} %bitcast.124), kind=kOutput, calls=%fused_computation.9 | convolution fusion | flops 50331648 | bytes 17302528 | tf_op jit(solution)/shard_map/ch,chpn->hpn/dot_general | solution.py:127
  479.6 37.1 %reduce-scatter.3.cloned.1.call-done = f32[16,128]{1,0:T(8,128)} async-done(((f32[128,128]{1,0:T(8,128)}), f32[16,128]{1,0:T(8,128)}) %reduce-scatter.3.cloned.1.call-update) | async-done | bytes 8208 | tf_op jit(solution)/shard_map/reduce_scatter | solution.py:144
  (102 shorter events, 32.1 us)
Async XLA Ops:
  7.2 102.9 %copy-start = (bf16[128,1024]{1,0:T(8,128)(2,1)S(1)}, bf16[128,1024]{1,0:T(8,128)(2,1)}, u32[]{:S(2)}) copy-start(bf16[128,1024]{1,0:T(8,128)(2,1)} %param.9) | copy-start | bytes 786436
  7.2 102.8 %all-gather.8.cloned.1.call-start = ((), (), s32[]{:S(2)}) async-start(), calls=%async_computation.3 | async-start | bytes 2162688 | tf_op jit(solution)/shard_map/all_gather | solution.py:81
  8.7 228.6 %all-gather.10.cloned.1.call-start = ((), (), s32[]{:S(2)}) async-start(), calls=%async_computation.6 | async-start | bytes 17301504 | tf_op jit(solution)/shard_map/all_gather | solution.py:22
  15.3 114.5 %all-to-all-start = ((f32[32,128,128]{2,1,0:T(8,128)}), f32[32,128,128]{2,1,0:T(8,128)}, u32[]{:S(2)}, u32[]{:S(2)}) async-start(f32[32,128,128]{2,1,0:T(8,128)} %stack.2), calls=%async_computation | async-start | bytes 4194304 | tf_op jit(solution)/shard_map/all_to_all | solution.py:17
  27.0 319.2 %reduce-scatter.5.cloned.1.call-start = ((), (), s32[]{:S(2)}) async-start(), calls=%async_computation.5 | async-start | bytes 73728 | tf_op jit(solution)/shard_map/reduce_scatter | solution.py:145
  120.0 5.7 %copy-start.1 = (f32[4096,128,8]{1,0,2:T(8,128)}, f32[4096,128,8]{1,0,2:T(8,128)S(1)}, u32[]{:S(2)}) copy-start(f32[4096,128,8]{1,0,2:T(8,128)S(1)} %get-tuple-element.164) | copy-start | bytes 50331652
  129.8 145.3 %copy-start.2 = (bf16[128,128]{1,0:T(8,128)(2,1)S(1)}, bf16[128,128]{1,0:T(8,128)(2,1)}, u32[]{:S(2)}) copy-start(bf16[128,128]{1,0:T(8,128)(2,1)} %param.14) | copy-start | bytes 98308
  129.8 147.0 %copy-start.3 = (bf16[128,128]{1,0:T(8,128)(2,1)S(1)}, bf16[128,128]{1,0:T(8,128)(2,1)}, u32[]{:S(2)}) copy-start(bf16[128,128]{1,0:T(8,128)(2,1)} %param.13) | copy-start | bytes 98308
  129.8 150.0 %copy-start.4 = (u32[256]{0:T(256)S(1)}, u32[256]{0:T(256)}, u32[]{:S(2)}) copy-start(u32[256]{0:T(256)} %constant.52) | copy-start | bytes 3076
  277.7 176.7 %all-gather.12.cloned.1.call-start = ((), (), s32[]{:S(2)}) async-start(), calls=%async_computation.7 | async-start | bytes 17301504 | tf_op jit(solution)/shard_map/all_gather | solution.py:121
  279.7 237.0 %reduce-scatter.3.cloned.1.call-start = ((), (), s32[]{:S(2)}) async-start(), calls=%async_computation.4 | async-start | bytes 73728 | tf_op jit(solution)/shard_map/reduce_scatter | solution.py:144
Sparse Core Ops, SparseCore 0:
  10.8 87.6 all-gather.7
  101.9 135.3 all-gather.9
  277.8 38.3 reduce-scatter.4
  319.8 134.4 all-gather.11
  478.3 38.3 reduce-scatter.2
